TPU v7x, 128 devices: a whole 4x4x4 slice. The times are simulated.
128 devices in a mesh: loop: 64 (over x, z, y), grp: 2 (over core).
Axes of the slice: x: 4, y: 4, z: 4, core: 2. Of those that a mesh axis runs over, the one named last changes fastest.
Arguments:
- particles: bfloat16 [8192, 3456], P('loop'), may hold values from -32 to 32
- references: bfloat16 [256, 3456], P(('loop', 'grp')), may hold values from -6 to 6
- classes: int32 [8192], P(('loop', 'grp')), may hold values from 0 to 255, as said below
- angles: int32 [8192], P(('loop', 'grp')), may hold values from 0 to 71
- weights: int32 [8192], P(('loop', 'grp')), may hold values from 1 to 4
Outputs:
- log_evidence: float32 [8192], P(('loop', 'grp'))
- class_average: float32 [256, 3456], P(('loop', 'grp'))
Inputs may be any that keep to these rules, and one draw needn't show every extreme that they name: Call the classes c with the same value of c // 4 the classes of one owner. In each aligned block of 64 rows at most 2 particles name the classes of one owner, and one owner receives exactly 2 from every block. Every class is named by some particle.
All inputs are finite; a program needn't handle non-finite values.
Results may differ from a plain program's by a relative error of at most 0.0003.
Values may be sent and summed in bfloat16 or wider, within the bound.
No kernel may reach another device: no remote copies, remote signals or barrier semaphores. Data moves between devices by JAX's collectives and lax.ppermute only.
A program may use at most 128 MiB of HBM per device.

v0:
```python
import math
import jax
import jax.numpy as jnp
from jax import lax
from jax.sharding import PartitionSpec as P

RADII = 48
ANGLES = 72
score_factor = 2.0


def turned_rows(ref_block, radius_count, angle_count):
    block_rows = ref_block.shape[0]
    polar_rows = ref_block.reshape(block_rows, radius_count, angle_count)
    angle_grid = jnp.arange(angle_count, dtype=jnp.int32)
    source_index = (angle_grid[:, None] + angle_grid[None, :]) % angle_count
    rotated = jnp.take(polar_rows, source_index, axis=2)
    rotated = jnp.transpose(rotated, (0, 2, 1, 3))
    return rotated.reshape(block_rows * angle_count, radius_count * angle_count)


def group_of():
    for group_size in (16, 8, 4, 2):
        return group_size
    return 1


def empty_stats(row_count):
    return (jnp.full((row_count,), -jnp.inf, jnp.float32), jnp.zeros((row_count,), jnp.float32))


def score_all(images, gathered):
    flat_len = images.shape[1]
    score_scale = score_factor / math.sqrt(flat_len)
    ref_count = gathered.shape[0]
    group_size = group_of()
    ref_groups = gathered.reshape(ref_count // group_size, group_size, flat_len)

    def advance(current, ref_block):
        highest, summed = current
        rotated = turned_rows(ref_block, RADII, ANGLES)
        scores = (
            lax.dot_general(
                images, rotated, (((1,), (1,)), ((), ())), preferred_element_type=jnp.float32
            )
            * score_scale
        )
        new_max = jnp.maximum(highest, jnp.max(scores, axis=1))
        summed = summed * jnp.exp(highest - new_max) + jnp.sum(
            jnp.exp(scores - new_max[:, None]), axis=1
        )
        return ((new_max, summed), None)

    result, _ = lax.scan(advance, empty_stats(images.shape[0]), ref_groups)
    return result


def local(particles, references, classes, angles, weights):
    row_count, flat_len = particles.shape
    grp_size = lax.axis_size("grp")
    half_rows = row_count // grp_size
    grp_index = lax.axis_index("grp")
    own_rows = lax.dynamic_slice_in_dim(particles, grp_index * half_rows, half_rows, 0)
    gathered = lax.all_gather(references, "loop", axis=0, tiled=True)
    highest, summed = score_all(particles, gathered)
    joint_max = lax.pmax(highest, "grp")
    summed = lax.psum(summed * jnp.exp(highest - joint_max), "grp")
    highest = joint_max
    highest = lax.dynamic_slice_in_dim(highest, grp_index * half_rows, half_rows, 0)
    summed = lax.dynamic_slice_in_dim(summed, grp_index * half_rows, half_rows, 0)
    log_evidence = highest + jnp.log(summed)
    owner_count = lax.axis_size("loop")
    per_owner = references.shape[0] * grp_size
    capacity = max(2, row_count // owner_count)
    slot_count = owner_count * capacity
    owner_of = classes // per_owner
    member_of = classes % per_owner
    owner_hits = (owner_of[:, None] == jnp.arange(owner_count, dtype=jnp.int32)[None, :]).astype(
        jnp.int32
    )
    earlier = jnp.cumsum(owner_hits, axis=0) - owner_hits
    slot_index = jnp.sum(earlier * owner_hits, axis=1)
    target_slot = owner_of * capacity + slot_index
    placement = (jnp.arange(slot_count, dtype=jnp.int32)[:, None] == target_slot[None, :]).astype(
        jnp.bfloat16
    )
    outgoing = jnp.dot(placement, own_rows, preferred_element_type=jnp.float32).astype(jnp.bfloat16)
    outgoing = outgoing.reshape(owner_count, capacity, flat_len)
    labels = jnp.stack([member_of, angles, weights], axis=1).astype(jnp.bfloat16)
    labels_out = jnp.dot(placement, labels, preferred_element_type=jnp.float32).astype(jnp.bfloat16)
    labels_out = labels_out.reshape(owner_count, capacity, 3)
    incoming, labels_in = (
        lax.all_to_all(outgoing, "loop", split_axis=0, concat_axis=0, tiled=True),
        lax.all_to_all(labels_out, "loop", split_axis=0, concat_axis=0, tiled=True),
    )
    images = incoming.reshape(slot_count, RADII, ANGLES)
    labels_in = labels_in.reshape(slot_count, 3).astype(jnp.float32)
    member_in = labels_in[:, 0]
    rotation = labels_in[:, 1]
    weight_of = labels_in[:, 2]
    angle_grid = jnp.arange(ANGLES, dtype=jnp.float32)
    source_angle = jnp.mod(angle_grid[None, :] - rotation[:, None], float(ANGLES))
    rotator = (angle_grid[None, :, None] == source_angle[:, None, :]).astype(jnp.bfloat16)
    aligned = jnp.einsum("srt,stf->srf", images, rotator, preferred_element_type=jnp.float32)
    aligned = aligned.astype(jnp.bfloat16).reshape(slot_count, flat_len)
    member_grid = jnp.arange(per_owner, dtype=jnp.float32)
    weighted = (
        (member_grid[:, None] == member_in[None, :]).astype(jnp.float32) * weight_of[None, :]
    ).astype(jnp.bfloat16)
    partial_sums = jnp.dot(weighted, aligned, preferred_element_type=jnp.float32)
    partial_weight = jnp.sum(weighted.astype(jnp.float32), axis=1)
    class_sums, class_weight = (
        lax.psum_scatter(partial_sums, "grp", scatter_dimension=0, tiled=True),
        lax.psum_scatter(partial_weight, "grp", scatter_dimension=0, tiled=True),
    )
    class_average = class_sums / class_weight[:, None]
    return (log_evidence, class_average)


def solution(mesh):
    return jax.shard_map(
        local,
        mesh=mesh,
        in_specs=(
            P("loop", None),
            P(("loop", "grp"), None),
            P(("loop", "grp")),
            P(("loop", "grp")),
            P(("loop", "grp")),
        ),
        out_specs=(P(("loop", "grp")), P(("loop", "grp"), None)),
        check_vma=False,
    )
```

profile of v0, /device:TPU:1, one launch (start us, length us, event | category | flops | bytes accessed | tf_op | source)
XLA Modules:
  0.0 887.3 jit_solution(3810419134806905992)
XLA Ops:
  3.2 12.2 %all-to-all-start = ((bf16[64,2,3]{2,1,0:T(2,128)(2,1)}), bf16[64,2,3]{2,1,0:T(2,128)(2,1)}, u32[]{:S(2)}, u32[]{:S(2)}) async-start(bf16[64,2,3]{2,1,0:T(2,128)(2,1)} %bitcast.4), calls=%async_computation | async-start | bytes 65536 | tf_op jit(solution)/shard_map/all_to_all | solution.py:94
  15.5 153.3 %all-gather = bf16[64,2,3456]{2,1,0:T(2,128)(2,1)S(1)} all-gather(bf16[1,2,3456]{2,1,0:T(2,128)(2,1)} %bitcast.39), channel_id=1, replica_groups=mesh['loop'=64,'grp'=2] {'loop'}, dimensions={0}, use_global_device_ids=true | all-gather | bytes 898560 | tf_op jit(solution)/shard_map/all_gather | solution.py:64
  169.2 649.2 %while.15 = (s32[]{:T(128)}, f32[128]{0:T(128)S(1)}, f32[128]{0:T(128)S(1)}, bf16[8,16,3456]{2,1,0:T(8,128)(2,1)S(1)}, bf16[128,3456]{1,0:T(8,128)(2,1)}, /*index=5*/s32[]{:T(128)}, s32[]{:T(128)}) while((s32[]{:T(128)}, f32[128]{0:T(128)S(1)}, f32[128]{0:T(128)S(1)}, bf16[8,16,3456]{2,1,0:T(8,128)(2,1)S(1)}, ...), condition=%wide.region_3.4_spmd.clone, body=%wide.region_0.3_spmd.clone.sunk | while | flops 1023913024 | bytes 78075904 | solution.py:54
  170.0 16.7 %gather_fusion = bf16[5184,16,48]{2,1,0:T(8,128)(2,1)} fusion(bf16[16,48,72]{1,0,2:T(8,128)(2,1)S(1)} %copy.31, s32[6144]{0:T(1024)S(1)} %pad_clamp_fusion.2), kind=kCustom, calls=%fused_computation.clone.clone.1 | custom fusion | bytes 15945984 | tf_op jit(solution)/shard_map/while/body/eval_jaxpr/jit(_take)/gather | solution.py:17
  186.8 24.6 %copy.32 = bf16[72,72,16,48]{1,3,0,2:T(8,128)(2,1)} copy(bf16[72,72,16,48]{3,2,1,0:T(8,128)(2,1)} %bitcast.37) | data formatting | bytes 15925248 | tf_op jit(solution)/shard_map/while/body/eval_jaxpr/jit(_take)/gather | solution.py:17
  211.4 10.6 %select_bitcast_fusion.2 = bf16[16,72,48,72]{3,2,1,0:T(8,128)(2,1)} fusion(bf16[72,72,16,48]{1,3,0,2:T(8,128)(2,1)} %copy.32, pred[72,72]{1,0:T(8,128)(4,1)S(1)} %compare_and_fusion.2), kind=kLoop, calls=%fused_computation.1.clone.1 | loop fusion | flops 3981312 | bytes 15930432 | tf_op jit(solution)/shard_map/while/body/eval_jaxpr/jit(_take)/select_n | solution.py:17
  222.1 22.6 %reshape.157 = bf16[1152,3456]{1,0:T(8,128)(2,1)} reshape(bf16[16,72,48,72]{3,2,1,0:T(8,128)(2,1)} %select_bitcast_fusion.2) | data formatting | bytes 15925248 | tf_op jit(solution)/shard_map/while/body/eval_jaxpr/reshape | solution.py:19
  244.6 5.5 fusion.45
  251.2 16.7 %gather_fusion = bf16[5184,16,48]{2,1,0:T(8,128)(2,1)} fusion(bf16[16,48,72]{1,0,2:T(8,128)(2,1)S(1)} %copy.31, s32[6144]{0:T(1024)S(1)} %pad_clamp_fusion.2), kind=kCustom, calls=%fused_computation.clone.clone.1 | custom fusion | bytes 15945984 | tf_op jit(solution)/shard_map/while/body/eval_jaxpr/jit(_take)/gather | solution.py:17
  267.9 24.6 %copy.32 = bf16[72,72,16,48]{1,3,0,2:T(8,128)(2,1)} copy(bf16[72,72,16,48]{3,2,1,0:T(8,128)(2,1)} %bitcast.37) | data formatting | bytes 15925248 | tf_op jit(solution)/shard_map/while/body/eval_jaxpr/jit(_take)/gather | solution.py:17
  292.6 10.6 %select_bitcast_fusion.2 = bf16[16,72,48,72]{3,2,1,0:T(8,128)(2,1)} fusion(bf16[72,72,16,48]{1,3,0,2:T(8,128)(2,1)} %copy.32, pred[72,72]{1,0:T(8,128)(4,1)S(1)} %compare_and_fusion.2), kind=kLoop, calls=%fused_computation.1.clone.1 | loop fusion | flops 3981312 | bytes 15930432 | tf_op jit(solution)/shard_map/while/body/eval_jaxpr/jit(_take)/select_n | solution.py:17
  303.2 22.6 %reshape.157 = bf16[1152,3456]{1,0:T(8,128)(2,1)} reshape(bf16[16,72,48,72]{3,2,1,0:T(8,128)(2,1)} %select_bitcast_fusion.2) | data formatting | bytes 15925248 | tf_op jit(solution)/shard_map/while/body/eval_jaxpr/reshape | solution.py:19
  325.8 5.5 fusion.45
  332.3 16.7 %gather_fusion = bf16[5184,16,48]{2,1,0:T(8,128)(2,1)} fusion(bf16[16,48,72]{1,0,2:T(8,128)(2,1)S(1)} %copy.31, s32[6144]{0:T(1024)S(1)} %pad_clamp_fusion.2), kind=kCustom, calls=%fused_computation.clone.clone.1 | custom fusion | bytes 15945984 | tf_op jit(solution)/shard_map/while/body/eval_jaxpr/jit(_take)/gather | solution.py:17
  349.1 24.6 %copy.32 = bf16[72,72,16,48]{1,3,0,2:T(8,128)(2,1)} copy(bf16[72,72,16,48]{3,2,1,0:T(8,128)(2,1)} %bitcast.37) | data formatting | bytes 15925248 | tf_op jit(solution)/shard_map/while/body/eval_jaxpr/jit(_take)/gather | solution.py:17
  373.7 10.6 %select_bitcast_fusion.2 = bf16[16,72,48,72]{3,2,1,0:T(8,128)(2,1)} fusion(bf16[72,72,16,48]{1,3,0,2:T(8,128)(2,1)} %copy.32, pred[72,72]{1,0:T(8,128)(4,1)S(1)} %compare_and_fusion.2), kind=kLoop, calls=%fused_computation.1.clone.1 | loop fusion | flops 3981312 | bytes 15930432 | tf_op jit(solution)/shard_map/while/body/eval_jaxpr/jit(_take)/select_n | solution.py:17
  384.4 22.6 %reshape.157 = bf16[1152,3456]{1,0:T(8,128)(2,1)} reshape(bf16[16,72,48,72]{3,2,1,0:T(8,128)(2,1)} %select_bitcast_fusion.2) | data formatting | bytes 15925248 | tf_op jit(solution)/shard_map/while/body/eval_jaxpr/reshape | solution.py:19
  407.0 5.5 fusion.45
  413.5 16.7 %gather_fusion = bf16[5184,16,48]{2,1,0:T(8,128)(2,1)} fusion(bf16[16,48,72]{1,0,2:T(8,128)(2,1)S(1)} %copy.31, s32[6144]{0:T(1024)S(1)} %pad_clamp_fusion.2), kind=kCustom, calls=%fused_computation.clone.clone.1 | custom fusion | bytes 15945984 | tf_op jit(solution)/shard_map/while/body/eval_jaxpr/jit(_take)/gather | solution.py:17
  430.2 24.6 %copy.32 = bf16[72,72,16,48]{1,3,0,2:T(8,128)(2,1)} copy(bf16[72,72,16,48]{3,2,1,0:T(8,128)(2,1)} %bitcast.37) | data formatting | bytes 15925248 | tf_op jit(solution)/shard_map/while/body/eval_jaxpr/jit(_take)/gather | solution.py:17
  454.9 10.6 %select_bitcast_fusion.2 = bf16[16,72,48,72]{3,2,1,0:T(8,128)(2,1)} fusion(bf16[72,72,16,48]{1,3,0,2:T(8,128)(2,1)} %copy.32, pred[72,72]{1,0:T(8,128)(4,1)S(1)} %compare_and_fusion.2), kind=kLoop, calls=%fused_computation.1.clone.1 | loop fusion | flops 3981312 | bytes 15930432 | tf_op jit(solution)/shard_map/while/body/eval_jaxpr/jit(_take)/select_n | solution.py:17
  465.5 22.6 %reshape.157 = bf16[1152,3456]{1,0:T(8,128)(2,1)} reshape(bf16[16,72,48,72]{3,2,1,0:T(8,128)(2,1)} %select_bitcast_fusion.2) | data formatting | bytes 15925248 | tf_op jit(solution)/shard_map/while/body/eval_jaxpr/reshape | solution.py:19
  488.1 5.5 fusion.45
  494.6 16.7 %gather_fusion = bf16[5184,16,48]{2,1,0:T(8,128)(2,1)} fusion(bf16[16,48,72]{1,0,2:T(8,128)(2,1)S(1)} %copy.31, s32[6144]{0:T(1024)S(1)} %pad_clamp_fusion.2), kind=kCustom, calls=%fused_computation.clone.clone.1 | custom fusion | bytes 15945984 | tf_op jit(solution)/shard_map/while/body/eval_jaxpr/jit(_take)/gather | solution.py:17
  511.4 24.6 %copy.32 = bf16[72,72,16,48]{1,3,0,2:T(8,128)(2,1)} copy(bf16[72,72,16,48]{3,2,1,0:T(8,128)(2,1)} %bitcast.37) | data formatting | bytes 15925248 | tf_op jit(solution)/shard_map/while/body/eval_jaxpr/jit(_take)/gather | solution.py:17
  536.1 10.6 %select_bitcast_fusion.2 = bf16[16,72,48,72]{3,2,1,0:T(8,128)(2,1)} fusion(bf16[72,72,16,48]{1,3,0,2:T(8,128)(2,1)} %copy.32, pred[72,72]{1,0:T(8,128)(4,1)S(1)} %compare_and_fusion.2), kind=kLoop, calls=%fused_computation.1.clone.1 | loop fusion | flops 3981312 | bytes 15930432 | tf_op jit(solution)/shard_map/while/body/eval_jaxpr/jit(_take)/select_n | solution.py:17
  546.7 22.6 %reshape.157 = bf16[1152,3456]{1,0:T(8,128)(2,1)} reshape(bf16[16,72,48,72]{3,2,1,0:T(8,128)(2,1)} %select_bitcast_fusion.2) | data formatting | bytes 15925248 | tf_op jit(solution)/shard_map/while/body/eval_jaxpr/reshape | solution.py:19
  569.3 5.5 fusion.45
  575.8 16.7 %gather_fusion = bf16[5184,16,48]{2,1,0:T(8,128)(2,1)} fusion(bf16[16,48,72]{1,0,2:T(8,128)(2,1)S(1)} %copy.31, s32[6144]{0:T(1024)S(1)} %pad_clamp_fusion.2), kind=kCustom, calls=%fused_computation.clone.clone.1 | custom fusion | bytes 15945984 | tf_op jit(solution)/shard_map/while/body/eval_jaxpr/jit(_take)/gather | solution.py:17
  592.5 24.6 %copy.32 = bf16[72,72,16,48]{1,3,0,2:T(8,128)(2,1)} copy(bf16[72,72,16,48]{3,2,1,0:T(8,128)(2,1)} %bitcast.37) | data formatting | bytes 15925248 | tf_op jit(solution)/shard_map/while/body/eval_jaxpr/jit(_take)/gather | solution.py:17
  617.2 10.6 %select_bitcast_fusion.2 = bf16[16,72,48,72]{3,2,1,0:T(8,128)(2,1)} fusion(bf16[72,72,16,48]{1,3,0,2:T(8,128)(2,1)} %copy.32, pred[72,72]{1,0:T(8,128)(4,1)S(1)} %compare_and_fusion.2), kind=kLoop, calls=%fused_computation.1.clone.1 | loop fusion | flops 3981312 | bytes 15930432 | tf_op jit(solution)/shard_map/while/body/eval_jaxpr/jit(_take)/select_n | solution.py:17
  627.8 22.6 %reshape.157 = bf16[1152,3456]{1,0:T(8,128)(2,1)} reshape(bf16[16,72,48,72]{3,2,1,0:T(8,128)(2,1)} %select_bitcast_fusion.2) | data formatting | bytes 15925248 | tf_op jit(solution)/shard_map/while/body/eval_jaxpr/reshape | solution.py:19
  650.4 5.5 fusion.45
  656.9 16.7 %gather_fusion = bf16[5184,16,48]{2,1,0:T(8,128)(2,1)} fusion(bf16[16,48,72]{1,0,2:T(8,128)(2,1)S(1)} %copy.31, s32[6144]{0:T(1024)S(1)} %pad_clamp_fusion.2), kind=kCustom, calls=%fused_computation.clone.clone.1 | custom fusion | bytes 15945984 | tf_op jit(solution)/shard_map/while/body/eval_jaxpr/jit(_take)/gather | solution.py:17
  673.7 24.6 %copy.32 = bf16[72,72,16,48]{1,3,0,2:T(8,128)(2,1)} copy(bf16[72,72,16,48]{3,2,1,0:T(8,128)(2,1)} %bitcast.37) | data formatting | bytes 15925248 | tf_op jit(solution)/shard_map/while/body/eval_jaxpr/jit(_take)/gather | solution.py:17
  698.4 10.6 %select_bitcast_fusion.2 = bf16[16,72,48,72]{3,2,1,0:T(8,128)(2,1)} fusion(bf16[72,72,16,48]{1,3,0,2:T(8,128)(2,1)} %copy.32, pred[72,72]{1,0:T(8,128)(4,1)S(1)} %compare_and_fusion.2), kind=kLoop, calls=%fused_computation.1.clone.1 | loop fusion | flops 3981312 | bytes 15930432 | tf_op jit(solution)/shard_map/while/body/eval_jaxpr/jit(_take)/select_n | solution.py:17
  709.0 22.6 %reshape.157 = bf16[1152,3456]{1,0:T(8,128)(2,1)} reshape(bf16[16,72,48,72]{3,2,1,0:T(8,128)(2,1)} %select_bitcast_fusion.2) | data formatting | bytes 15925248 | tf_op jit(solution)/shard_map/while/body/eval_jaxpr/reshape | solution.py:19
  731.6 5.5 fusion.45
  738.1 16.7 %gather_fusion = bf16[5184,16,48]{2,1,0:T(8,128)(2,1)} fusion(bf16[16,48,72]{1,0,2:T(8,128)(2,1)S(1)} %copy.31, s32[6144]{0:T(1024)S(1)} %pad_clamp_fusion.2), kind=kCustom, calls=%fused_computation.clone.clone.1 | custom fusion | bytes 15945984 | tf_op jit(solution)/shard_map/while/body/eval_jaxpr/jit(_take)/gather | solution.py:17
  754.9 24.6 %copy.32 = bf16[72,72,16,48]{1,3,0,2:T(8,128)(2,1)} copy(bf16[72,72,16,48]{3,2,1,0:T(8,128)(2,1)} %bitcast.37) | data formatting | bytes 15925248 | tf_op jit(solution)/shard_map/while/body/eval_jaxpr/jit(_take)/gather | solution.py:17
  779.5 10.6 %select_bitcast_fusion.2 = bf16[16,72,48,72]{3,2,1,0:T(8,128)(2,1)} fusion(bf16[72,72,16,48]{1,3,0,2:T(8,128)(2,1)} %copy.32, pred[72,72]{1,0:T(8,128)(4,1)S(1)} %compare_and_fusion.2), kind=kLoop, calls=%fused_computation.1.clone.1 | loop fusion | flops 3981312 | bytes 15930432 | tf_op jit(solution)/shard_map/while/body/eval_jaxpr/jit(_take)/select_n | solution.py:17
  790.2 22.6 %reshape.157 = bf16[1152,3456]{1,0:T(8,128)(2,1)} reshape(bf16[16,72,48,72]{3,2,1,0:T(8,128)(2,1)} %select_bitcast_fusion.2) | data formatting | bytes 15925248 | tf_op jit(solution)/shard_map/while/body/eval_jaxpr/reshape | solution.py:19
  812.7 5.5 fusion.45
  821.1 31.1 %pmax.7 = f32[128]{0:T(128)S(1)} all-reduce(f32[128]{0:T(128)S(1)} %get-tuple-element.69), channel_id=1, replica_groups=mesh['loop'=64,'grp'=2] {'grp'}, use_global_device_ids=true, to_apply=%region_4.5 | all-reduce | flops 128 | bytes 1024 | tf_op jit(solution)/shard_map/pmax | solution.py:66
  852.2 4.6 all-to-all-start.1
  859.5 13.0 %all-to-all-done.1 = bf16[64,2,3456]{2,1,0:T(2,128)(2,1)S(1)} async-done(((bf16[64,2,3456]{2,1,0:T(2,128)(2,1)}), bf16[64,2,3456]{2,1,0:T(2,128)(2,1)S(1)}, u32[]{:S(2)}, u32[]{:S(2)}) %all-to-all-start.1) | async-done | bytes 884768 | tf_op jit(solution)/shard_map/all_to_all | solution.py:93
  872.5 3.4 reshape.125
  880.4 5.5 all-reduce.2
  (139 shorter events, 21.4 us)
Async XLA Ops:
  1.7 13.8 %copy-start.1 = (s32[64]{0:T(128)}, s32[64]{0:T(128)S(1)}, u32[]{:S(2)}) copy-start(s32[64]{0:T(128)S(1)} %multiply_add_fusion) | copy-start | bytes 772
  3.2 849.0 %all-to-all-start = ((bf16[64,2,3]{2,1,0:T(2,128)(2,1)}), bf16[64,2,3]{2,1,0:T(2,128)(2,1)}, u32[]{:S(2)}, u32[]{:S(2)}) async-start(bf16[64,2,3]{2,1,0:T(2,128)(2,1)} %bitcast.4), calls=%async_computation | async-start | bytes 65536 | tf_op jit(solution)/shard_map/all_to_all | solution.py:94
  169.2 649.3 %copy-start.2 = (s32[64]{0:T(128)S(1)}, s32[64]{0:T(128)}, u32[]{:S(2)}) copy-start(s32[64]{0:T(128)} %copy-done.1) | copy-start | bytes 772
  169.2 687.7 %copy-start.3 = (u32[128]{0:T(128)S(1)}, u32[128]{0:T(128)}, u32[]{:S(2)}) copy-start(u32[128]{0:T(128)} %constant.129) | copy-start | bytes 1540
  222.1 22.6 %copy-start = (bf16[128,3456]{1,0:T(8,128)(2,1)S(1)}, bf16[128,3456]{1,0:T(8,128)(2,1)}, u32[]{:S(2)}) copy-start(bf16[128,3456]{1,0:T(8,128)(2,1)} %get-tuple-element.163) | copy-start | bytes 2654212 | tf_op jit(solution)/shard_map/while
  303.2 22.6 %copy-start = (bf16[128,3456]{1,0:T(8,128)(2,1)S(1)}, bf16[128,3456]{1,0:T(8,128)(2,1)}, u32[]{:S(2)}) copy-start(bf16[128,3456]{1,0:T(8,128)(2,1)} %get-tuple-element.163) | copy-start | bytes 2654212 | tf_op jit(solution)/shard_map/while
  384.4 22.6 %copy-start = (bf16[128,3456]{1,0:T(8,128)(2,1)S(1)}, bf16[128,3456]{1,0:T(8,128)(2,1)}, u32[]{:S(2)}) copy-start(bf16[128,3456]{1,0:T(8,128)(2,1)} %get-tuple-element.163) | copy-start | bytes 2654212 | tf_op jit(solution)/shard_map/while
  465.5 22.6 %copy-start = (bf16[128,3456]{1,0:T(8,128)(2,1)S(1)}, bf16[128,3456]{1,0:T(8,128)(2,1)}, u32[]{:S(2)}) copy-start(bf16[128,3456]{1,0:T(8,128)(2,1)} %get-tuple-element.163) | copy-start | bytes 2654212 | tf_op jit(solution)/shard_map/while
  546.7 22.6 %copy-start = (bf16[128,3456]{1,0:T(8,128)(2,1)S(1)}, bf16[128,3456]{1,0:T(8,128)(2,1)}, u32[]{:S(2)}) copy-start(bf16[128,3456]{1,0:T(8,128)(2,1)} %get-tuple-element.163) | copy-start | bytes 2654212 | tf_op jit(solution)/shard_map/while
  627.8 22.6 %copy-start = (bf16[128,3456]{1,0:T(8,128)(2,1)S(1)}, bf16[128,3456]{1,0:T(8,128)(2,1)}, u32[]{:S(2)}) copy-start(bf16[128,3456]{1,0:T(8,128)(2,1)} %get-tuple-element.163) | copy-start | bytes 2654212 | tf_op jit(solution)/shard_map/while
  709.0 22.6 %copy-start = (bf16[128,3456]{1,0:T(8,128)(2,1)S(1)}, bf16[128,3456]{1,0:T(8,128)(2,1)}, u32[]{:S(2)}) copy-start(bf16[128,3456]{1,0:T(8,128)(2,1)} %get-tuple-element.163) | copy-start | bytes 2654212 | tf_op jit(solution)/shard_map/while
  790.2 22.6 %copy-start = (bf16[128,3456]{1,0:T(8,128)(2,1)S(1)}, bf16[128,3456]{1,0:T(8,128)(2,1)}, u32[]{:S(2)}) copy-start(bf16[128,3456]{1,0:T(8,128)(2,1)} %get-tuple-element.163) | copy-start | bytes 2654212 | tf_op jit(solution)/shard_map/while
  852.2 20.4 %all-to-all-start.1 = ((bf16[64,2,3456]{2,1,0:T(2,128)(2,1)}), bf16[64,2,3456]{2,1,0:T(2,128)(2,1)S(1)}, u32[]{:S(2)}, u32[]{:S(2)}) async-start(bf16[64,2,3456]{2,1,0:T(2,128)(2,1)} %reshape.124), calls=%async_computation.1 | async-start | bytes 1769472 | tf_op jit(solution)/shard_map/all_to_all | solution.py:93
where the time goes:
time: 897 us; the launch traced here: 887 us
  local copies, waits for them, and re-layouts  527 us (59%)
  blocking collectives  190 us (21%)
  other arithmetic  90.5 us (10%)
  matrix products  48 us (5%)
  starting transfers between devices  16.9 us (2%)
  waiting for transfers between devices  13 us (1%)
    gather x16, local copies, waits for them, and re-layouts, turned_rows(): rotated = jnp.take(polar_rows, source_index, axis=2)  331 us
    reshape x8, local copies, waits for them, and re-layouts, turned_rows(): return rotated.reshape(block_rows * angle_count, radius_count * angle_count)  181 us
    all_gather x1, blocking collectives, local(): gathered = lax.all_gather(references, 'loop', axis=0, tiled=True)  153 us
    select_n x16, other arithmetic, turned_rows(): rotated = jnp.take(polar_rows, source_index, axis=2)  85.3 us
    dot_general x8, matrix products, advance(): lax.dot_general(images, rotated, (((1,), (1,)), ((), ())), preferred_elem...  44 us
    pmax x1, blocking collectives, local(): joint_max = lax.pmax(highest, 'grp')  31.1 us
  transfers between devices with their start and end apart: 2, of which 1 were waited for; matrix products, arithmetic and copies ran while one was open for 74% of the time, Pallas kernels for 0%

commit v1 on v0

--- a/solution.py
+++ b/solution.py
@@ -61,7 +61,9 @@
     half_rows = row_count // grp_size
     grp_index = lax.axis_index("grp")
     own_rows = lax.dynamic_slice_in_dim(particles, grp_index * half_rows, half_rows, 0)
-    gathered = lax.all_gather(references, "loop", axis=0, tiled=True)
+    gathered = jnp.concatenate(
+        lax.all_to_all(jnp.stack([references] * lax.axis_size("loop")), "loop", 0, 0), axis=0
+    )
     highest, summed = score_all(particles, gathered)
     joint_max = lax.pmax(highest, "grp")
     summed = lax.psum(summed * jnp.exp(highest - joint_max), "grp")

time: 897 us -> 727 us (0.81)
  blocking collectives: 190 us -> 9.39 us
    all_gather x1 -> x0, blocking collectives: 153 us -> none  [local(): gathered = lax.all_gather(references, 'loop', axis=0, tiled=True)]
    pmax x1, blocking collectives: 31.1 us -> 5.65 us  [local(): joint_max = lax.pmax(highest, 'grp')]
    all_to_all x1, waiting for transfers between devices: 13 us -> 0.01 us  [local(): lax.all_to_all(outgoing, 'loop', split_axis=0, concat_axis=0, tiled=True)]
  transfers between devices with their start and end apart: 2 -> 3, of which waited for: 1 -> 2; matrix products, arithmetic and copies ran while one was open for 74% -> 91% of each run, Pallas kernels for 0% -> 0%
where the time goes in v1:
time: 727 us; the launch traced here: 717 us
  local copies, waits for them, and re-layouts  529 us (73%)
  other arithmetic  91.7 us (13%)
  matrix products  46.9 us (6%)
  starting transfers between devices  22.1 us (3%)
  waiting for transfers between devices  16.5 us (2%)
  blocking collectives  9.39 us (1%)
    gather x16, local copies, waits for them, and re-layouts, turned_rows(): rotated = jnp.take(polar_rows, source_index, axis=2)  331 us
    reshape x8, local copies, waits for them, and re-layouts, turned_rows(): return rotated.reshape(block_rows * angle_count, radius_count * angle_count)  180 us
    select_n x16, other arithmetic, turned_rows(): rotated = jnp.take(polar_rows, source_index, axis=2)  85.3 us
    dot_general x8, matrix products, advance(): lax.dot_general(images, rotated, (((1,), (1,)), ((), ())), preferred_elem...  44 us
  transfers between devices with their start and end apart: 3, of which 2 were waited for; matrix products, arithmetic and copies ran while one was open for 91% of the time, Pallas kernels for 0%

profile of v1, /device:TPU:1, one launch (start us, length us, event | category | flops | bytes accessed | tf_op | source)
XLA Modules:
  0.0 717.4 jit_solution(16062217362010633349)
XLA Ops:
  3.3 12.0 %all-to-all-start.1 = ((bf16[64,2,3]{2,1,0:T(2,128)(2,1)}), bf16[64,2,3]{2,1,0:T(2,128)(2,1)S(1)}, u32[]{:S(2)}, u32[]{:S(2)}) async-start(bf16[64,2,3]{2,1,0:T(2,128)(2,1)} %bitcast.3), calls=%async_computation.1 | async-start | bytes 65536 | tf_op jit(solution)/shard_map/all_to_all | solution.py:96
  15.3 8.4 %all-to-all-done.1 = bf16[64,2,3]{2,1,0:T(2,128)(2,1)S(1)} async-done(((bf16[64,2,3]{2,1,0:T(2,128)(2,1)}), bf16[64,2,3]{2,1,0:T(2,128)(2,1)S(1)}, u32[]{:S(2)}, u32[]{:S(2)}) %all-to-all-start.1) | async-done | bytes 800 | tf_op jit(solution)/shard_map/all_to_all | solution.py:96
  25.8 4.7 all-to-all-start
  36.8 8.1 %all-to-all-done = bf16[64,2,3456]{2,1,0:T(2,128)(2,1)S(1)} async-done(((bf16[64,2,3456]{2,1,0:T(2,128)(2,1)}), bf16[64,2,3456]{2,1,0:T(2,128)(2,1)S(1)}, u32[]{:S(2)}, u32[]{:S(2)}) %all-to-all-start) | async-done | bytes 884768 | tf_op jit(solution)/shard_map/all_to_all | solution.py:65
  44.9 5.5 all-to-all-start.2
  50.8 648.6 %while.15 = (s32[]{:T(128)}, f32[128]{0:T(128)S(1)}, f32[128]{0:T(128)S(1)}, bf16[8,16,3456]{2,1,0:T(8,128)(2,1)S(1)}, bf16[128,3456]{1,0:T(8,128)(2,1)S(1)}, /*index=5*/s32[]{:T(128)}, s32[]{:T(128)}) while((s32[]{:T(128)}, f32[128]{0:T(128)S(1)}, f32[128]{0:T(128)S(1)}, bf16[8,16,3456]{2,1,0:T(8,128)(2,1)S(1)}, ...), condition=%wide.region_3.4_spmd.clone, body=%wide.region_0.3_spmd.clone.sunk | while | flops 1023913024 | bytes 74536928 | solution.py:54
  51.6 16.7 %gather_fusion = bf16[5184,16,48]{2,1,0:T(8,128)(2,1)} fusion(bf16[16,48,72]{1,0,2:T(8,128)(2,1)S(1)} %copy.31, s32[6144]{0:T(1024)S(1)} %pad_clamp_fusion.2), kind=kCustom, calls=%fused_computation.clone.clone.1 | custom fusion | bytes 15945984 | tf_op jit(solution)/shard_map/while/body/eval_jaxpr/jit(_take)/gather | solution.py:17
  68.4 24.6 %copy.32 = bf16[72,72,16,48]{1,3,0,2:T(8,128)(2,1)} copy(bf16[72,72,16,48]{3,2,1,0:T(8,128)(2,1)} %bitcast.36) | data formatting | bytes 15925248 | tf_op jit(solution)/shard_map/while/body/eval_jaxpr/jit(_take)/gather | solution.py:17
  93.0 10.6 %select_bitcast_fusion.2 = bf16[16,72,48,72]{3,2,1,0:T(8,128)(2,1)} fusion(bf16[72,72,16,48]{1,3,0,2:T(8,128)(2,1)} %copy.32, pred[72,72]{1,0:T(8,128)(4,1)S(1)} %compare_and_fusion.2), kind=kLoop, calls=%fused_computation.1.clone.1 | loop fusion | flops 3981312 | bytes 15930432 | tf_op jit(solution)/shard_map/while/body/eval_jaxpr/jit(_take)/select_n | solution.py:17
  103.7 22.5 %reshape.152 = bf16[1152,3456]{1,0:T(8,128)(2,1)} reshape(bf16[16,72,48,72]{3,2,1,0:T(8,128)(2,1)} %select_bitcast_fusion.2) | data formatting | bytes 15925248 | tf_op jit(solution)/shard_map/while/body/eval_jaxpr/reshape | solution.py:19
  126.2 5.5 fusion.45
  132.7 16.7 %gather_fusion = bf16[5184,16,48]{2,1,0:T(8,128)(2,1)} fusion(bf16[16,48,72]{1,0,2:T(8,128)(2,1)S(1)} %copy.31, s32[6144]{0:T(1024)S(1)} %pad_clamp_fusion.2), kind=kCustom, calls=%fused_computation.clone.clone.1 | custom fusion | bytes 15945984 | tf_op jit(solution)/shard_map/while/body/eval_jaxpr/jit(_take)/gather | solution.py:17
  149.4 24.6 %copy.32 = bf16[72,72,16,48]{1,3,0,2:T(8,128)(2,1)} copy(bf16[72,72,16,48]{3,2,1,0:T(8,128)(2,1)} %bitcast.36) | data formatting | bytes 15925248 | tf_op jit(solution)/shard_map/while/body/eval_jaxpr/jit(_take)/gather | solution.py:17
  174.1 10.6 %select_bitcast_fusion.2 = bf16[16,72,48,72]{3,2,1,0:T(8,128)(2,1)} fusion(bf16[72,72,16,48]{1,3,0,2:T(8,128)(2,1)} %copy.32, pred[72,72]{1,0:T(8,128)(4,1)S(1)} %compare_and_fusion.2), kind=kLoop, calls=%fused_computation.1.clone.1 | loop fusion | flops 3981312 | bytes 15930432 | tf_op jit(solution)/shard_map/while/body/eval_jaxpr/jit(_take)/select_n | solution.py:17
  184.7 22.5 %reshape.152 = bf16[1152,3456]{1,0:T(8,128)(2,1)} reshape(bf16[16,72,48,72]{3,2,1,0:T(8,128)(2,1)} %select_bitcast_fusion.2) | data formatting | bytes 15925248 | tf_op jit(solution)/shard_map/while/body/eval_jaxpr/reshape | solution.py:19
  207.2 5.5 fusion.45
  213.8 16.7 %gather_fusion = bf16[5184,16,48]{2,1,0:T(8,128)(2,1)} fusion(bf16[16,48,72]{1,0,2:T(8,128)(2,1)S(1)} %copy.31, s32[6144]{0:T(1024)S(1)} %pad_clamp_fusion.2), kind=kCustom, calls=%fused_computation.clone.clone.1 | custom fusion | bytes 15945984 | tf_op jit(solution)/shard_map/while/body/eval_jaxpr/jit(_take)/gather | solution.py:17
  230.5 24.6 %copy.32 = bf16[72,72,16,48]{1,3,0,2:T(8,128)(2,1)} copy(bf16[72,72,16,48]{3,2,1,0:T(8,128)(2,1)} %bitcast.36) | data formatting | bytes 15925248 | tf_op jit(solution)/shard_map/while/body/eval_jaxpr/jit(_take)/gather | solution.py:17
  255.2 10.6 %select_bitcast_fusion.2 = bf16[16,72,48,72]{3,2,1,0:T(8,128)(2,1)} fusion(bf16[72,72,16,48]{1,3,0,2:T(8,128)(2,1)} %copy.32, pred[72,72]{1,0:T(8,128)(4,1)S(1)} %compare_and_fusion.2), kind=kLoop, calls=%fused_computation.1.clone.1 | loop fusion | flops 3981312 | bytes 15930432 | tf_op jit(solution)/shard_map/while/body/eval_jaxpr/jit(_take)/select_n | solution.py:17
  265.8 22.5 %reshape.152 = bf16[1152,3456]{1,0:T(8,128)(2,1)} reshape(bf16[16,72,48,72]{3,2,1,0:T(8,128)(2,1)} %select_bitcast_fusion.2) | data formatting | bytes 15925248 | tf_op jit(solution)/shard_map/while/body/eval_jaxpr/reshape | solution.py:19
  288.3 5.5 fusion.45
  294.8 16.7 %gather_fusion = bf16[5184,16,48]{2,1,0:T(8,128)(2,1)} fusion(bf16[16,48,72]{1,0,2:T(8,128)(2,1)S(1)} %copy.31, s32[6144]{0:T(1024)S(1)} %pad_clamp_fusion.2), kind=kCustom, calls=%fused_computation.clone.clone.1 | custom fusion | bytes 15945984 | tf_op jit(solution)/shard_map/while/body/eval_jaxpr/jit(_take)/gather | solution.py:17
  311.6 24.6 %copy.32 = bf16[72,72,16,48]{1,3,0,2:T(8,128)(2,1)} copy(bf16[72,72,16,48]{3,2,1,0:T(8,128)(2,1)} %bitcast.36) | data formatting | bytes 15925248 | tf_op jit(solution)/shard_map/while/body/eval_jaxpr/jit(_take)/gather | solution.py:17
  336.2 10.6 %select_bitcast_fusion.2 = bf16[16,72,48,72]{3,2,1,0:T(8,128)(2,1)} fusion(bf16[72,72,16,48]{1,3,0,2:T(8,128)(2,1)} %copy.32, pred[72,72]{1,0:T(8,128)(4,1)S(1)} %compare_and_fusion.2), kind=kLoop, calls=%fused_computation.1.clone.1 | loop fusion | flops 3981312 | bytes 15930432 | tf_op jit(solution)/shard_map/while/body/eval_jaxpr/jit(_take)/select_n | solution.py:17
  346.9 22.5 %reshape.152 = bf16[1152,3456]{1,0:T(8,128)(2,1)} reshape(bf16[16,72,48,72]{3,2,1,0:T(8,128)(2,1)} %select_bitcast_fusion.2) | data formatting | bytes 15925248 | tf_op jit(solution)/shard_map/while/body/eval_jaxpr/reshape | solution.py:19
  369.4 5.5 fusion.45
  375.9 16.7 %gather_fusion = bf16[5184,16,48]{2,1,0:T(8,128)(2,1)} fusion(bf16[16,48,72]{1,0,2:T(8,128)(2,1)S(1)} %copy.31, s32[6144]{0:T(1024)S(1)} %pad_clamp_fusion.2), kind=kCustom, calls=%fused_computation.clone.clone.1 | custom fusion | bytes 15945984 | tf_op jit(solution)/shard_map/while/body/eval_jaxpr/jit(_take)/gather | solution.py:17
  392.6 24.6 %copy.32 = bf16[72,72,16,48]{1,3,0,2:T(8,128)(2,1)} copy(bf16[72,72,16,48]{3,2,1,0:T(8,128)(2,1)} %bitcast.36) | data formatting | bytes 15925248 | tf_op jit(solution)/shard_map/while/body/eval_jaxpr/jit(_take)/gather | solution.py:17
  417.3 10.6 %select_bitcast_fusion.2 = bf16[16,72,48,72]{3,2,1,0:T(8,128)(2,1)} fusion(bf16[72,72,16,48]{1,3,0,2:T(8,128)(2,1)} %copy.32, pred[72,72]{1,0:T(8,128)(4,1)S(1)} %compare_and_fusion.2), kind=kLoop, calls=%fused_computation.1.clone.1 | loop fusion | flops 3981312 | bytes 15930432 | tf_op jit(solution)/shard_map/while/body/eval_jaxpr/jit(_take)/select_n | solution.py:17
  427.9 22.5 %reshape.152 = bf16[1152,3456]{1,0:T(8,128)(2,1)} reshape(bf16[16,72,48,72]{3,2,1,0:T(8,128)(2,1)} %select_bitcast_fusion.2) | data formatting | bytes 15925248 | tf_op jit(solution)/shard_map/while/body/eval_jaxpr/reshape | solution.py:19
  450.4 5.5 fusion.45
  457.0 16.7 %gather_fusion = bf16[5184,16,48]{2,1,0:T(8,128)(2,1)} fusion(bf16[16,48,72]{1,0,2:T(8,128)(2,1)S(1)} %copy.31, s32[6144]{0:T(1024)S(1)} %pad_clamp_fusion.2), kind=kCustom, calls=%fused_computation.clone.clone.1 | custom fusion | bytes 15945984 | tf_op jit(solution)/shard_map/while/body/eval_jaxpr/jit(_take)/gather | solution.py:17
  473.7 24.6 %copy.32 = bf16[72,72,16,48]{1,3,0,2:T(8,128)(2,1)} copy(bf16[72,72,16,48]{3,2,1,0:T(8,128)(2,1)} %bitcast.36) | data formatting | bytes 15925248 | tf_op jit(solution)/shard_map/while/body/eval_jaxpr/jit(_take)/gather | solution.py:17
  498.4 10.6 %select_bitcast_fusion.2 = bf16[16,72,48,72]{3,2,1,0:T(8,128)(2,1)} fusion(bf16[72,72,16,48]{1,3,0,2:T(8,128)(2,1)} %copy.32, pred[72,72]{1,0:T(8,128)(4,1)S(1)} %compare_and_fusion.2), kind=kLoop, calls=%fused_computation.1.clone.1 | loop fusion | flops 3981312 | bytes 15930432 | tf_op jit(solution)/shard_map/while/body/eval_jaxpr/jit(_take)/select_n | solution.py:17
  509.0 22.5 %reshape.152 = bf16[1152,3456]{1,0:T(8,128)(2,1)} reshape(bf16[16,72,48,72]{3,2,1,0:T(8,128)(2,1)} %select_bitcast_fusion.2) | data formatting | bytes 15925248 | tf_op jit(solution)/shard_map/while/body/eval_jaxpr/reshape | solution.py:19
  531.5 5.5 fusion.45
  538.0 16.7 %gather_fusion = bf16[5184,16,48]{2,1,0:T(8,128)(2,1)} fusion(bf16[16,48,72]{1,0,2:T(8,128)(2,1)S(1)} %copy.31, s32[6144]{0:T(1024)S(1)} %pad_clamp_fusion.2), kind=kCustom, calls=%fused_computation.clone.clone.1 | custom fusion | bytes 15945984 | tf_op jit(solution)/shard_map/while/body/eval_jaxpr/jit(_take)/gather | solution.py:17
  554.8 24.6 %copy.32 = bf16[72,72,16,48]{1,3,0,2:T(8,128)(2,1)} copy(bf16[72,72,16,48]{3,2,1,0:T(8,128)(2,1)} %bitcast.36) | data formatting | bytes 15925248 | tf_op jit(solution)/shard_map/while/body/eval_jaxpr/jit(_take)/gather | solution.py:17
  579.4 10.6 %select_bitcast_fusion.2 = bf16[16,72,48,72]{3,2,1,0:T(8,128)(2,1)} fusion(bf16[72,72,16,48]{1,3,0,2:T(8,128)(2,1)} %copy.32, pred[72,72]{1,0:T(8,128)(4,1)S(1)} %compare_and_fusion.2), kind=kLoop, calls=%fused_computation.1.clone.1 | loop fusion | flops 3981312 | bytes 15930432 | tf_op jit(solution)/shard_map/while/body/eval_jaxpr/jit(_take)/select_n | solution.py:17
  590.1 22.5 %reshape.152 = bf16[1152,3456]{1,0:T(8,128)(2,1)} reshape(bf16[16,72,48,72]{3,2,1,0:T(8,128)(2,1)} %select_bitcast_fusion.2) | data formatting | bytes 15925248 | tf_op jit(solution)/shard_map/while/body/eval_jaxpr/reshape | solution.py:19
  612.6 5.5 fusion.45
  619.1 16.7 %gather_fusion = bf16[5184,16,48]{2,1,0:T(8,128)(2,1)} fusion(bf16[16,48,72]{1,0,2:T(8,128)(2,1)S(1)} %copy.31, s32[6144]{0:T(1024)S(1)} %pad_clamp_fusion.2), kind=kCustom, calls=%fused_computation.clone.clone.1 | custom fusion | bytes 15945984 | tf_op jit(solution)/shard_map/while/body/eval_jaxpr/jit(_take)/gather | solution.py:17
  635.9 24.6 %copy.32 = bf16[72,72,16,48]{1,3,0,2:T(8,128)(2,1)} copy(bf16[72,72,16,48]{3,2,1,0:T(8,128)(2,1)} %bitcast.36) | data formatting | bytes 15925248 | tf_op jit(solution)/shard_map/while/body/eval_jaxpr/jit(_take)/gather | solution.py:17
  660.5 10.6 %select_bitcast_fusion.2 = bf16[16,72,48,72]{3,2,1,0:T(8,128)(2,1)} fusion(bf16[72,72,16,48]{1,3,0,2:T(8,128)(2,1)} %copy.32, pred[72,72]{1,0:T(8,128)(4,1)S(1)} %compare_and_fusion.2), kind=kLoop, calls=%fused_computation.1.clone.1 | loop fusion | flops 3981312 | bytes 15930432 | tf_op jit(solution)/shard_map/while/body/eval_jaxpr/jit(_take)/select_n | solution.py:17
  671.2 22.5 %reshape.152 = bf16[1152,3456]{1,0:T(8,128)(2,1)} reshape(bf16[16,72,48,72]{3,2,1,0:T(8,128)(2,1)} %select_bitcast_fusion.2) | data formatting | bytes 15925248 | tf_op jit(solution)/shard_map/while/body/eval_jaxpr/reshape | solution.py:19
  693.6 5.5 fusion.45
  699.4 5.6 pmax.7
  705.0 4.8 reshape.123
  (133 shorter events, 26.2 us)
Async XLA Ops:
  0.6 50.1 %copy-start = (bf16[128,3456]{1,0:T(8,128)(2,1)S(1)}, bf16[128,3456]{1,0:T(8,128)(2,1)}, u32[]{:S(2)}) copy-start(bf16[128,3456]{1,0:T(8,128)(2,1)} %param.7) | copy-start | bytes 2654212
  3.3 20.4 %all-to-all-start.1 = ((bf16[64,2,3]{2,1,0:T(2,128)(2,1)}), bf16[64,2,3]{2,1,0:T(2,128)(2,1)S(1)}, u32[]{:S(2)}, u32[]{:S(2)}) async-start(bf16[64,2,3]{2,1,0:T(2,128)(2,1)} %bitcast.3), calls=%async_computation.1 | async-start | bytes 65536 | tf_op jit(solution)/shard_map/all_to_all | solution.py:96
  25.8 19.2 %all-to-all-start = ((bf16[64,2,3456]{2,1,0:T(2,128)(2,1)}), bf16[64,2,3456]{2,1,0:T(2,128)(2,1)S(1)}, u32[]{:S(2)}, u32[]{:S(2)}) async-start(bf16[64,2,3456]{2,1,0:T(2,128)(2,1)} %stack.14), calls=%async_computation | async-start | bytes 1769472 | tf_op jit(solution)/shard_map/all_to_all | solution.py:65
  35.4 15.4 %copy-start.5 = (bf16[128]{0:T(256)(128)(2,1)}, bf16[128]{0:T(256)(128)(2,1)S(1)}, u32[]{:S(2)}) copy-start(bf16[128]{0:T(256)(128)(2,1)S(1)} %slice_bitcast_fusion.1) | copy-start | bytes 772
  35.4 15.4 %copy-start.2 = (f32[128]{0:T(128)}, f32[128]{0:T(128)S(1)}, u32[]{:S(2)}) copy-start(f32[128]{0:T(128)S(1)} %get-tuple-element.104) | copy-start | bytes 1540
  44.9 660.1 %all-to-all-start.2 = ((bf16[64,2,3456]{2,1,0:T(2,128)(2,1)}), bf16[64,2,3456]{2,1,0:T(2,128)(2,1)}, u32[]{:S(2)}, u32[]{:S(2)}) async-start(bf16[64,2,3456]{2,1,0:T(2,128)(2,1)} %reshape.122), calls=%async_computation.2 | async-start | bytes 1769472 | tf_op jit(solution)/shard_map/all_to_all | solution.py:95
  50.8 659.1 %copy-start.1 = (f32[128,72]{1,0:T(8,128)S(1)}, f32[128,72]{1,0:T(8,128)}, u32[]{:S(2)}) copy-start(f32[128,72]{1,0:T(8,128)} %add_select_fusion.2) | copy-start | bytes 110596
  699.4 12.5 %copy-start.3 = (f32[128]{0:T(128)S(1)}, f32[128]{0:T(128)}, u32[]{:S(2)}) copy-start(f32[128]{0:T(128)} %copy-done.2) | copy-start | bytes 1540
  699.4 12.5 %copy-start.6 = (bf16[128]{0:T(256)(128)(2,1)S(1)}, bf16[128]{0:T(256)(128)(2,1)}, u32[]{:S(2)}) copy-start(bf16[128]{0:T(256)(128)(2,1)} %copy-done.5) | copy-start | bytes 772
  699.4 12.9 %copy-start.4 = (f32[4]{0:T(128)S(1)}, f32[4]{0:T(128)}, u32[]{:S(2)}) copy-start(f32[4]{0:T(128)} %convert_reduce_fusion) | copy-start | bytes 52
